TPU v7x, 128 devices: a whole 4x4x4 slice. The times are simulated.
128 devices in a mesh: region: 8 (over x, core), unit: 16 (over y, z).
Axes of the slice: x: 4, y: 4, z: 4, core: 2. Of those that a mesh axis runs over, the one named last changes fastest.
Arguments:
- noisy: bfloat16 [32768, 2048], P(('region', 'unit')), may hold values from -6 to 6
- strategy: bfloat16 [2048, 2048], replicated, may hold values from -0.125 to 0.125
- county_hist: float32 [1024, 2048], P(('region', 'unit')), may hold values from -24 to 24
- tract_county: int32 [32768], P(('region', 'unit')), may hold values from 0 to 1023, as said below
- tract_owner: int32 [32768, 1], P(('region', 'unit')), may hold values from 0 to 127; in each aligned block of 256 rows (0 to 255, 256 to 511, ...) at most 4 rows name the same one
Outputs:
- released: bfloat16 [32768, 2048], P(('region', 'unit'))
- relaid: float32 [65536, 2048], P(('region', 'unit'))
Inputs may be any that keep to these rules, and one draw needn't show every extreme that they name: `tract_county`: every county has at least one tract; the tracts of region r (rows r * 256 * 16 onward) lie in counties of region r (rows r * 8 * 16 onward of county_hist). `tract_owner`: among the 256 rows of one device no owner appears more than 4 times, and some owner appears exactly 4 times.
All inputs are finite; a program needn't handle non-finite values.
Results may differ from a plain program's by a relative error of at most 0.005.
Values sent between devices are 32-bit elements; how exact they have to be, the bound alone decides.
No kernel may reach another device: no remote copies, remote signals or barrier semaphores. Data moves between devices by JAX's collectives and lax.ppermute only.
A program may use at most 64 MiB of HBM per device.

v0:
```python
import jax
import jax.numpy as jnp
from jax import lax
from jax.sharding import PartitionSpec as P

ITERS = 2
step_size = 0.25


def local(noisy, strategy, county_hist, tract_county, tract_owner):
    unit_count = lax.axis_size("unit")
    region_count = lax.axis_size("region")
    devices = region_count * unit_count
    tract_rows = noisy.shape[0]
    width = strategy.shape[0]
    county_region = county_hist.shape[0] * unit_count
    first_county = lax.axis_index("region") * county_region
    local_id = tract_county - first_county
    member = (local_id[:, None] == jnp.arange(county_region, dtype=jnp.int32)[None, :]).astype(
        jnp.float32
    )
    county_tally = jnp.sum(member, axis=0)
    estimate = jnp.zeros((tract_rows, width), jnp.float32)
    for iteration in range(ITERS):
        if iteration == 0:
            misfit = -noisy
        else:
            answers = jnp.dot(
                estimate.astype(jnp.bfloat16), strategy, preferred_element_type=jnp.float32
            )
            misfit = (answers - noisy.astype(jnp.float32)).astype(jnp.bfloat16)
        gradient = lax.dot_general(
            misfit, strategy, (((1,), (1,)), ((), ())), preferred_element_type=jnp.float32
        )
        stepped = estimate - step_size * gradient
        partial_value = lax.dot_general(
            member,
            stepped,
            (((0,), (0,)), ((), ())),
            precision=lax.Precision.HIGHEST,
            preferred_element_type=jnp.float32,
        )
        child_total, tract_count = (
            lax.psum_scatter(partial_value, "unit", scatter_dimension=0, tiled=True),
            lax.psum_scatter(county_tally, "unit", scatter_dimension=0, tiled=True),
        )
        parent_gap = (county_hist - child_total) / tract_count[:, None]
        region_gap = lax.all_gather(parent_gap, "unit", axis=0, tiled=True)
        estimate = stepped + jnp.dot(
            member, region_gap, precision=lax.Precision.HIGHEST, preferred_element_type=jnp.float32
        )
    owners = tract_owner[:, 0]
    owner_hits = (owners[:, None] == jnp.arange(devices, dtype=jnp.int32)[None, :]).astype(
        jnp.int32
    )
    slot_index = jnp.sum((jnp.cumsum(owner_hits, axis=0) - owner_hits) * owner_hits, axis=1)
    capacity = 2 * tract_rows // devices
    target = owners * capacity + slot_index
    outgoing = jnp.zeros((devices * capacity, width), jnp.float32).at[target].set(estimate)
    released = jnp.dot(
        estimate.astype(jnp.bfloat16), strategy, preferred_element_type=jnp.float32
    ).astype(jnp.bfloat16)
    grouped = outgoing.reshape(devices, capacity, width)
    arrived = lax.all_to_all(grouped, ("region", "unit"), split_axis=0, concat_axis=0, tiled=True)
    relaid = arrived.reshape(devices * capacity, width)
    return (released, relaid)


def solution(mesh):
    in_specs = (
        P(("region", "unit"), None),
        P(),
        P(("region", "unit"), None),
        P(("region", "unit")),
        P(("region", "unit"), None),
    )
    out_specs = (P(("region", "unit"), None), P(("region", "unit"), None))
    return jax.shard_map(local, mesh=mesh, in_specs=in_specs, out_specs=out_specs, check_vma=False)
```

profile of v0, /device:TPU:6, one launch (start us, length us, event | category | flops | bytes accessed | tf_op | source)
XLA Modules:
  0.0 385.6 jit_solution(13782813712799772541)
XLA Ops:
  7.2 0.7 broadcast_subtract_fusion
  7.9 6.1 %fusion = f32[256,2048]{1,0:T(8,128)S(1)} fusion(bf16[2048,2048]{1,0:T(8,128)(2,1)} %param.6, bf16[256,2048]{1,0:T(8,128)(2,1)} %param.5), kind=kOutput, calls=%fused_computation.5 | convolution fusion | flops 2149056512 | bytes 11534336 | tf_op jit(solution)/shard_map/dot_general | solution.py:32
  14.0 1.9 fusion.15
  16.0 0.6 dynamic-slice
  17.4 42.1 %all-reduce.1 = f32[128]{0:T(128)S(1)} all-reduce(f32[128]{0:T(128)S(1)} %convert_reduce_fusion), channel_id=3, replica_groups=mesh['region'=8,'unit'=16] {'unit'}, use_global_device_ids=true, to_apply=%region_2.0.clone | all-reduce | flops 128 | bytes 1024
  59.5 46.5 %all-reduce.6.cloned.1.call-done = f32[128,2048]{1,0:T(8,128)} async-done(((f32[128,2048]{1,0:T(8,128)}), f32[128,2048]{1,0:T(8,128)}) %all-reduce.6.cloned.1.call-update) | async-done | bytes 1048592
  106.0 1.5 fusion.17
  107.6 42.9 %all-gather.3.cloned.1.call-done = f32[128,2048]{1,0:T(8,128)} async-done(((f32[8,2048]{1,0:T(8,128)}), f32[128,2048]{1,0:T(8,128)}) %all-gather.3.cloned.1.call-update) | async-done | bytes 1048592 | tf_op jit(solution)/shard_map/all_gather | solution.py:48
  150.5 3.6 convolution_add_fusion.1
  154.1 11.5 %fusion.1 = f32[256,2048]{1,0:T(8,128)S(1)} fusion(f32[256,2048]{1,0:T(8,128)} %convolution_add_fusion.1, bf16[2048,2048]{1,0:T(8,128)(2,1)} %param.6, bf16[256,2048]{1,0:T(8,128)(2,1)S(1)} %copy-done.3), kind=kOutput, calls=%fused_computation.6 | convolution fusion | flops 4298113024 | bytes 13631488 | tf_op jit(solution)/shard_map/dot_general | solution.py:32
  165.6 1.9 fusion.14
  167.5 0.2 all-gather.5.cloned.1.call-start
  167.7 86.7 %all-reduce.8.cloned.1.call-done = f32[128,2048]{1,0:T(8,128)} async-done(((f32[128,2048]{1,0:T(8,128)}), f32[128,2048]{1,0:T(8,128)}) %all-reduce.8.cloned.1.call-update) | async-done | bytes 1048592
  254.4 1.5 fusion.16
  256.1 0.2 fusion.10
  256.4 0.2 fusion.12
  256.6 42.2 %all-gather.5.cloned.1.call-done = f32[128,2048]{1,0:T(8,128)} async-done(((f32[8,2048]{1,0:T(8,128)}), f32[128,2048]{1,0:T(8,128)}) %all-gather.5.cloned.1.call-update) | async-done | bytes 1048592 | tf_op jit(solution)/shard_map/all_gather | solution.py:48
  298.8 3.6 convolution_add_fusion
  302.4 5.1 %scatter_custom_fusion = f32[512,2048]{1,0:T(8,128)} fusion(s32[256]{0:T(256)S(1)} %bitcast.33, f32[256,2048]{1,0:T(8,128)} %convolution_add_fusion, f32[]{:T(128)} %constant.8.clone.1), kind=kCustom, calls=%fused_computation.10 | custom fusion | bytes 4194816 | tf_op jit(solution)/shard_map/scatter | solution.py:59
  307.6 5.2 %reshape.30 = f32[128,4,2048]{2,1,0:T(4,128)} reshape(f32[512,2048]{1,0:T(8,128)} %scatter_custom_fusion) | data formatting | bytes 8388608 | tf_op jit(solution)/shard_map/reshape | solution.py:63
  312.7 7.8 %all-to-all-start = ((f32[128,4,2048]{2,1,0:T(4,128)}), f32[128,4,2048]{2,1,0:T(4,128)}, u32[]{:S(2)}, u32[]{:S(2)}) async-start(f32[128,4,2048]{2,1,0:T(4,128)} %reshape.30), calls=%async_computation | async-start | bytes 8388608 | tf_op jit(solution)/shard_map/all_to_all | solution.py:64
  320.6 6.7 %convolution_convert_fusion = bf16[256,2048]{1,0:T(8,128)(2,1)} fusion(bf16[2048,2048]{1,0:T(8,128)(2,1)} %param.6, f32[256,2048]{1,0:T(8,128)S(1)} %copy-done), kind=kOutput, calls=%fused_computation.9 | convolution fusion | flops 2148532224 | bytes 11534336 | tf_op jit(solution)/shard_map/dot_general | solution.py:60
  327.3 46.5 %all-to-all-done = f32[128,4,2048]{2,1,0:T(4,128)} async-done(((f32[128,4,2048]{2,1,0:T(4,128)}), f32[128,4,2048]{2,1,0:T(4,128)}, u32[]{:S(2)}, u32[]{:S(2)}) %all-to-all-start) | async-done | bytes 4194336 | tf_op jit(solution)/shard_map/all_to_all | solution.py:64
  373.8 5.3 %reshape.31 = f32[512,2048]{1,0:T(8,128)} reshape(f32[128,4,2048]{2,1,0:T(4,128)} %all-to-all-done) | data formatting | bytes 8388608 | tf_op jit(solution)/shard_map/reshape | solution.py:65
  (27 shorter events, 0.6 us)
Async XLA Ops:
  7.2 98.8 %all-reduce.6.cloned.1.call-start = ((), (), s32[]{:S(2)}) async-start(), calls=%async_computation.3 | async-start | bytes 2097152
  14.0 2.0 copy-start.4
  14.0 92.0 %copy-start.1 = (f32[8,2048]{1,0:T(8,128)S(1)}, f32[8,2048]{1,0:T(8,128)}, u32[]{:S(2)}) copy-start(f32[8,2048]{1,0:T(8,128)} %param.7) | copy-start | bytes 196612
  15.9 134.5 %all-gather.3.cloned.1.call-start = ((), (), s32[]{:S(2)}) async-start(), calls=%async_computation.1 | async-start | bytes 1114112 | tf_op jit(solution)/shard_map/all_gather | solution.py:48
  107.5 46.5 %copy-start.3 = (bf16[256,2048]{1,0:T(8,128)(2,1)S(1)}, bf16[256,2048]{1,0:T(8,128)(2,1)}, u32[]{:S(2)}) copy-start(bf16[256,2048]{1,0:T(8,128)(2,1)} %param.5) | copy-start | bytes 3145732
  107.5 146.9 %all-reduce.8.cloned.1.call-start = ((), (), s32[]{:S(2)}) async-start(), calls=%async_computation.4 | async-start | bytes 2097152
  165.6 90.4 %copy-start.2 = (s32[256,1]{0,1:T(1,128)S(1)}, s32[256,1]{0,1:T(1,128)}, u32[]{:S(2)}) copy-start(s32[256,1]{0,1:T(1,128)} %param.9) | copy-start | bytes 3076
  167.5 131.3 %all-gather.5.cloned.1.call-start = ((), (), s32[]{:S(2)}) async-start(), calls=%async_computation.2 | async-start | bytes 1114112 | tf_op jit(solution)/shard_map/all_gather | solution.py:48
  312.7 7.9 %copy-start = (f32[256,2048]{1,0:T(8,128)S(1)}, f32[256,2048]{1,0:T(8,128)}, u32[]{:S(2)}) copy-start(f32[256,2048]{1,0:T(8,128)} %convolution_add_fusion) | copy-start | bytes 6291460
  312.7 61.1 %all-to-all-start = ((f32[128,4,2048]{2,1,0:T(4,128)}), f32[128,4,2048]{2,1,0:T(4,128)}, u32[]{:S(2)}, u32[]{:S(2)}) async-start(f32[128,4,2048]{2,1,0:T(4,128)} %reshape.30), calls=%async_computation | async-start | bytes 8388608 | tf_op jit(solution)/shard_map/all_to_all | solution.py:64
Sparse Core Ops, SparseCore 0:
  16.1 89.8 all-reduce.5
  108.7 41.7 all-gather.2
  167.6 86.7 all-reduce.7
  257.0 41.7 all-gather.4
where the time goes:
time: 386 us
  waiting for transfers between devices  265 us (69%)
  blocking collectives  42.1 us (11%)
  matrix products  35.3 us (9%)
  local copies, waits for them, and re-layouts  16.4 us (4%)
  between operations  14.5 us (4%)
  starting transfers between devices  8.19 us (2%)
  other arithmetic  4.33 us (1%)
    unnamed x6, waiting for transfers between devices  133 us
    all_gather x2, waiting for transfers between devices, local(): region_gap = lax.all_gather(parent_gap, 'unit', axis=0, tiled=True)  85.1 us
    all_to_all x1, waiting for transfers between devices, local(): lax.all_to_all(grouped, ('region', 'unit'), split_axis=0, concat_axis=0,...  46.5 us
    unnamed x1, blocking collectives  42.1 us
    dot_general x2, matrix products, local(): lax.dot_general(misfit, strategy, (((1,), (1,)), ((), ())), preferred_ele...  17.6 us
    all_to_all x1, starting transfers between devices, local(): lax.all_to_all(grouped, ('region', 'unit'), split_axis=0, concat_axis=0,...  7.85 us
  transfers between devices with their start and end apart: 5, of which 5 were waited for; matrix products, arithmetic and copies ran while one was open for 2% of the time, Pallas kernels for 0%

commit v1 on v0

--- a/solution.py
+++ b/solution.py
@@ -45,7 +45,11 @@
             lax.psum_scatter(county_tally, "unit", scatter_dimension=0, tiled=True),
         )
         parent_gap = (county_hist - child_total) / tract_count[:, None]
-        region_gap = lax.all_gather(parent_gap, "unit", axis=0, tiled=True)
+        count = lax.axis_size("unit")
+        repeats = [count if d == 0 else 1 for d in range(parent_gap.ndim)]
+        region_gap = lax.all_to_all(
+            jnp.tile(parent_gap, repeats), "unit", split_axis=0, concat_axis=0, tiled=True
+        )
         estimate = stepped + jnp.dot(
             member, region_gap, precision=lax.Precision.HIGHEST, preferred_element_type=jnp.float32
         )

time: 386 us -> 335 us (0.87)
  waiting for transfers between devices: 265 us -> 193 us
  blocking collectives: 42.1 us -> 61.8 us
    all_gather x2 -> x0, waiting for transfers between devices: 85.1 us -> none  [local(): region_gap = lax.all_gather(parent_gap, 'unit', axis=0, tiled=True)]
    all_to_all x0 -> x1, blocking collectives: none -> 19.8 us  [local(): lax.all_to_all(jnp.tile(parent_gap, repeats), 'unit', split_axis=0, conca...]
    all_to_all x0 -> x1, waiting for transfers between devices: none -> 14.6 us  [local(): lax.all_to_all(jnp.tile(parent_gap, repeats), 'unit', split_axis=0, conca...]
    all_to_all x0 -> x1, starting transfers between devices: none -> 4.86 us  [local(): lax.all_to_all(jnp.tile(parent_gap, repeats), 'unit', split_axis=0, conca...]
    unnamed x6 -> x4, waiting for transfers between devices: 133 us -> 132 us
  transfers between devices with their start and end apart: 5 -> 4, of which waited for: 5 -> 4; matrix products, arithmetic and copies ran while one was open for 2% -> 2% of each run, Pallas kernels for 0% -> 0%
where the time goes in v1:
time: 335 us
  waiting for transfers between devices  193 us (58%)
  blocking collectives  61.8 us (18%)
  matrix products  32.9 us (10%)
  local copies, waits for them, and re-layouts  17.6 us (5%)
  between operations  14.8 us (4%)
  starting transfers between devices  11.4 us (3%)
    unnamed x4, waiting for transfers between devices  132 us
    all_to_all x1, waiting for transfers between devices, local(): lax.all_to_all(grouped, ('region', 'unit'), split_axis=0, concat_axis=0,...  46.5 us
    unnamed x1, blocking collectives  42.1 us
    all_to_all x1, blocking collectives, local(): lax.all_to_all(jnp.tile(parent_gap, repeats), 'unit', split_axis=0, conca...  19.8 us
    dot_general x2, matrix products, local(): lax.dot_general(misfit, strategy, (((1,), (1,)), ((), ())), preferred_ele...  17.6 us
    all_to_all x1, waiting for transfers between devices, local(): lax.all_to_all(jnp.tile(parent_gap, repeats), 'unit', split_axis=0, conca...  14.6 us
  transfers between devices with their start and end apart: 4, of which 4 were waited for; matrix products, arithmetic and copies ran while one was open for 2% of the time, Pallas kernels for 0%

profile of v1, /device:TPU:6, one launch (start us, length us, event | category | flops | bytes accessed | tf_op | source)
XLA Modules:
  0.0 334.5 jit_solution(17405523079297468950)
XLA Ops:
  7.2 0.7 broadcast_subtract_fusion
  7.9 6.1 %fusion = f32[256,2048]{1,0:T(8,128)S(1)} fusion(bf16[2048,2048]{1,0:T(8,128)(2,1)} %param.6, bf16[256,2048]{1,0:T(8,128)(2,1)} %param.5), kind=kOutput, calls=%fused_computation.5 | convolution fusion | flops 2149056512 | bytes 11534336 | tf_op jit(solution)/shard_map/dot_general | solution.py:32
  14.0 1.9 fusion.17
  16.0 0.6 dynamic-slice
  17.4 42.1 %all-reduce.1 = f32[128]{0:T(128)S(1)} all-reduce(f32[128]{0:T(128)S(1)} %convert_reduce_fusion), channel_id=3, replica_groups=mesh['region'=8,'unit'=16] {'unit'}, use_global_device_ids=true, to_apply=%region_2.0.clone | all-reduce | flops 128 | bytes 1024
  59.5 46.5 %all-reduce.6.cloned.1.call-done = f32[128,2048]{1,0:T(8,128)} async-done(((f32[128,2048]{1,0:T(8,128)}), f32[128,2048]{1,0:T(8,128)}) %all-reduce.6.cloned.1.call-update) | async-done | bytes 1048592
  106.0 0.9 fusion.19
  107.0 19.8 %all_to_all.23 = f32[16,8,2048]{2,1,0:T(8,128)S(1)} all-to-all(f32[16,8,2048]{2,1,0:T(8,128)S(1)} %tile.4), channel_id=1, replica_groups=mesh['region'=8,'unit'=16] {'unit'}, dimensions={0} | all-to-all | bytes 2097152 | tf_op jit(solution)/shard_map/all_to_all | solution.py:50
  126.7 2.4 convolution_add_fusion.1
  129.1 11.5 %fusion.1 = f32[256,2048]{1,0:T(8,128)S(1)} fusion(f32[256,2048]{1,0:T(8,128)} %convolution_add_fusion.1, bf16[2048,2048]{1,0:T(8,128)(2,1)} %param.6, bf16[256,2048]{1,0:T(8,128)(2,1)S(1)} %copy-done.3), kind=kOutput, calls=%fused_computation.6 | convolution fusion | flops 4298113024 | bytes 13631488 | tf_op jit(solution)/shard_map/dot_general | solution.py:32
  140.6 1.9 fusion.16
  142.7 85.3 %all-reduce.8.cloned.1.call-done = f32[128,2048]{1,0:T(8,128)} async-done(((f32[128,2048]{1,0:T(8,128)}), f32[128,2048]{1,0:T(8,128)}) %all-reduce.8.cloned.1.call-update) | async-done | bytes 1048592
  228.0 0.9 fusion.18
  228.9 1.1 tile.5
  230.0 4.9 %all-to-all-start.1 = ((f32[16,8,2048]{2,1,0:T(8,128)}), f32[16,8,2048]{2,1,0:T(8,128)S(1)}, u32[]{:S(2)}, u32[]{:S(2)}) async-start(f32[16,8,2048]{2,1,0:T(8,128)} %tile.5), calls=%async_computation.1 | async-start | bytes 2097152 | tf_op jit(solution)/shard_map/all_to_all | solution.py:50
  234.8 0.2 fusion.12
  235.3 14.6 %all-to-all-done.1 = f32[16,8,2048]{2,1,0:T(8,128)S(1)} async-done(((f32[16,8,2048]{2,1,0:T(8,128)}), f32[16,8,2048]{2,1,0:T(8,128)S(1)}, u32[]{:S(2)}, u32[]{:S(2)}) %all-to-all-start.1) | async-done | bytes 1048608 | tf_op jit(solution)/shard_map/all_to_all | solution.py:50
  250.0 2.4 convolution_add_fusion
  252.4 5.1 %scatter_custom_fusion = f32[512,2048]{1,0:T(8,128)} fusion(s32[256]{0:T(256)S(1)} %bitcast.37, f32[256,2048]{1,0:T(8,128)} %convolution_add_fusion, f32[]{:T(128)} %constant.8.clone.1), kind=kCustom, calls=%fused_computation.10 | custom fusion | bytes 4194816 | tf_op jit(solution)/shard_map/scatter | solution.py:63
  257.5 5.2 %reshape.44 = f32[128,4,2048]{2,1,0:T(4,128)} reshape(f32[512,2048]{1,0:T(8,128)} %scatter_custom_fusion) | data formatting | bytes 8388608 | tf_op jit(solution)/shard_map/reshape | solution.py:67
  262.7 6.5 %all-to-all-start.2 = ((f32[128,4,2048]{2,1,0:T(4,128)}), f32[128,4,2048]{2,1,0:T(4,128)}, u32[]{:S(2)}, u32[]{:S(2)}) async-start(f32[128,4,2048]{2,1,0:T(4,128)} %reshape.44), calls=%async_computation.2 | async-start | bytes 8388608 | tf_op jit(solution)/shard_map/all_to_all | solution.py:68
  269.2 6.7 %convolution_convert_fusion = bf16[256,2048]{1,0:T(8,128)(2,1)} fusion(bf16[2048,2048]{1,0:T(8,128)(2,1)} %param.6, f32[256,2048]{1,0:T(8,128)S(1)} %copy-done), kind=kOutput, calls=%fused_computation.9 | convolution fusion | flops 2148532224 | bytes 11534336 | tf_op jit(solution)/shard_map/dot_general | solution.py:64
  275.9 46.5 %all-to-all-done.2 = f32[128,4,2048]{2,1,0:T(4,128)} async-done(((f32[128,4,2048]{2,1,0:T(4,128)}), f32[128,4,2048]{2,1,0:T(4,128)}, u32[]{:S(2)}, u32[]{:S(2)}) %all-to-all-start.2) | async-done | bytes 4194336 | tf_op jit(solution)/shard_map/all_to_all | solution.py:68
  322.4 5.3 %reshape.45 = f32[512,2048]{1,0:T(8,128)} reshape(f32[128,4,2048]{2,1,0:T(4,128)} %all-to-all-done.2) | data formatting | bytes 8388608 | tf_op jit(solution)/shard_map/reshape | solution.py:69
  (26 shorter events, 0.8 us)
Async XLA Ops:
  7.2 98.8 %all-reduce.6.cloned.1.call-start = ((), (), s32[]{:S(2)}) async-start(), calls=%async_computation.3 | async-start | bytes 2097152
  14.0 2.0 copy-start.4
  14.0 92.0 %copy-start.1 = (f32[8,2048]{1,0:T(8,128)S(1)}, f32[8,2048]{1,0:T(8,128)}, u32[]{:S(2)}) copy-start(f32[8,2048]{1,0:T(8,128)} %param.7) | copy-start | bytes 196612
  15.9 212.0 %all-reduce.8.cloned.1.call-start = ((), (), s32[]{:S(2)}) async-start(), calls=%async_computation.4 | async-start | bytes 2097152
  126.7 2.4 copy-start.3
  140.6 1.9 copy-start.2
  230.0 20.0 %all-to-all-start.1 = ((f32[16,8,2048]{2,1,0:T(8,128)}), f32[16,8,2048]{2,1,0:T(8,128)S(1)}, u32[]{:S(2)}, u32[]{:S(2)}) async-start(f32[16,8,2048]{2,1,0:T(8,128)} %tile.5), calls=%async_computation.1 | async-start | bytes 2097152 | tf_op jit(solution)/shard_map/all_to_all | solution.py:50
  262.7 6.5 %copy-start = (f32[256,2048]{1,0:T(8,128)S(1)}, f32[256,2048]{1,0:T(8,128)}, u32[]{:S(2)}) copy-start(f32[256,2048]{1,0:T(8,128)} %convolution_add_fusion) | copy-start | bytes 6291460
  262.7 59.7 %all-to-all-start.2 = ((f32[128,4,2048]{2,1,0:T(4,128)}), f32[128,4,2048]{2,1,0:T(4,128)}, u32[]{:S(2)}, u32[]{:S(2)}) async-start(f32[128,4,2048]{2,1,0:T(4,128)} %reshape.44), calls=%async_computation.2 | async-start | bytes 8388608 | tf_op jit(solution)/shard_map/all_to_all | solution.py:68
Sparse Core Ops, SparseCore 0:
  16.1 89.8 all-reduce.5
  142.7 85.2 all-reduce.7
